TPU v7x, 128 devices: a whole 4x4x4 slice. The times are simulated.
128 devices in a mesh: grp: 8 (over z, core), dev: 16 (over y, x).
Axes of the slice: x: 4, y: 4, z: 4, core: 2. Of those that a mesh axis runs over, the one named last changes fastest.
Arguments:
- positions: float32 [3, 131072], P(None, ('grp', 'dev')), may hold values from -3 to 3
- velocities: float32 [3, 131072], P(None, ('grp', 'dev')), may hold values from -5 to 5
- accelerations: float32 [3, 131072], P(None, ('grp', 'dev')), may hold values from -3 to 3
- jerks: float32 [3, 131072], P(None, ('grp', 'dev')), may hold values from -3 to 3
- levels: int32 [131072], P(('grp', 'dev')), may hold values from 0 to 5
- counts: int32 [2, 128], replicated, may hold values from 1 to 256, 16384 in all within a row
- active_rows: int32 [2, 32768], P(None, ('grp', 'dev')), may hold values from 0 to 1023, as said below
Outputs:
- new_positions: float32 [3, 131072], P(None, ('grp', 'dev'))
- new_velocities: float32 [3, 131072], P(None, ('grp', 'dev'))
- new_accelerations: float32 [3, 131072], P(None, ('grp', 'dev'))
- new_jerks: float32 [3, 131072], P(None, ('grp', 'dev'))
Inputs may be any that keep to these rules, and one draw needn't show every extreme that they name: In each step the 128 counts sum to exactly 16384 and the largest of them is exactly 256. `active_rows`: for each step and device, the 256 entries of the device's slots are distinct indices of that device's own stars; only the first counts of them are live.
All inputs are finite; a program needn't handle non-finite values.
Results may differ from a plain program's by a relative error of at most 0.00022.
Values sent between devices are 32-bit elements; how exact they have to be, the bound alone decides.
No kernel may reach another device: no remote copies, remote signals or barrier semaphores. Data moves between devices by JAX's collectives and lax.ppermute only.
A program may use at most 128 MiB of HBM per device.

v0:
```python
import math

import jax
import jax.numpy as jnp
from jax import lax
from jax.experimental import pallas as pl
from jax.experimental.pallas import tpu as pltpu
from jax.sharding import PartitionSpec as P

tick_length = 1.0 / 128.0


LANES = 128
SUB = 8


def _pair_terms_kernel(cnt_ref, tgt_ref, src_ref, out_ref, acc_ref, *, soft_sq, mass, n_chunks, n_owner, slot_cap):
    acc_ref[...] = jnp.zeros(acc_ref.shape, jnp.float32)

    def one_group(base, n_half):
        tile = tgt_ref[pl.ds(base, n_half * SUB), :]
        halves = []
        for h in range(n_half):
            part = tile[h * SUB:(h + 1) * SUB, :]
            halves.append([jnp.broadcast_to(part[:, k:k + 1], (SUB, LANES)) for k in range(6)])

        def chunk(c, accs):
            off = pl.multiple_of(c * LANES, LANES)
            s = [src_ref[k, :, pl.ds(off, LANES)] for k in range(6)]
            new = []
            for h in range(n_half):
                t = halves[h]
                a = accs[6 * h:6 * h + 6]
                dx = s[0] - t[0]
                dy = s[1] - t[1]
                dz = s[2] - t[2]
                ux = s[3] - t[3]
                uy = s[4] - t[4]
                uz = s[5] - t[5]
                r2 = dx * dx + dy * dy + dz * dz + soft_sq
                inv = lax.rsqrt(r2)
                inv2 = inv * inv
                w = inv * inv2
                al = 3.0 * (dx * ux + dy * uy + dz * uz) * inv2
                new += [
                    a[0] + w * dx,
                    a[1] + w * dy,
                    a[2] + w * dz,
                    a[3] + w * (ux - al * dx),
                    a[4] + w * (uy - al * dy),
                    a[5] + w * (uz - al * dz),
                ]
            return tuple(new)

        zero = jnp.zeros((SUB, LANES), jnp.float32)
        accs = lax.fori_loop(0, n_chunks, chunk, (zero,) * (6 * n_half), unroll=16)
        for h in range(n_half):
            for k in range(6):
                total = jnp.sum(accs[6 * h + k], axis=1, keepdims=True) * mass
                acc_ref[pl.ds(base + h * SUB, SUB), pl.ds(k, 1)] = total

    def one_owner(o, carry):
        count = jnp.clip(cnt_ref[o], 0, slot_cap)
        n_full = count // (2 * SUB)
        rest = count - n_full * (2 * SUB)
        tail = pl.multiple_of(o * slot_cap + n_full * (2 * SUB), SUB)

        def body(gi, c):
            one_group(pl.multiple_of(o * slot_cap + gi * (2 * SUB), 2 * SUB), 2)
            return c

        lax.fori_loop(0, n_full, body, 0)

        @pl.when(rest > SUB)
        def _():
            one_group(tail, 2)

        @pl.when((rest > 0) & (rest <= SUB))
        def _():
            one_group(tail, 1)

        return carry

    lax.fori_loop(0, n_owner, one_owner, 0)

    def flip(o, carry):
        block = acc_ref[pl.ds(pl.multiple_of(o * slot_cap, slot_cap), slot_cap), :]
        out_ref[o] = block.T[:8, :]
        return carry

    lax.fori_loop(0, n_owner, flip, 0)


def pair_terms(col_counts, tgt, src, mass, soft_sq, interpret=False):
    cap = tgt.shape[0]
    n_owner = col_counts.shape[0]
    n_src = src.shape[1]
    src_b = jnp.broadcast_to(src[:, None, :], (6, SUB, n_src))
    kernel = lambda *refs: _pair_terms_kernel(
        *refs, soft_sq=soft_sq, mass=mass, n_chunks=n_src // LANES, n_owner=n_owner, slot_cap=cap // n_owner
    )
    return pl.pallas_call(
        kernel,
        out_shape=jax.ShapeDtypeStruct((n_owner, 8, cap // n_owner), jnp.float32),
        in_specs=[
            pl.BlockSpec(memory_space=pltpu.SMEM),
            pl.BlockSpec(memory_space=pltpu.VMEM),
            pl.BlockSpec(memory_space=pltpu.VMEM),
        ],
        out_specs=pl.BlockSpec(memory_space=pltpu.VMEM),
        scratch_shapes=[pltpu.VMEM((cap, LANES), jnp.float32)],
        interpret=interpret,
    )(col_counts.astype(jnp.int32), tgt, src_b)


def pair_block(targets, src_pos, src_vel, mass, soft_sq):
    gap_x = src_pos[0][None, :] - targets[0][:, None]
    gap_y = src_pos[1][None, :] - targets[1][:, None]
    gap_z = src_pos[2][None, :] - targets[2][:, None]
    drift_x = src_vel[0][None, :] - targets[3][:, None]
    drift_y = src_vel[1][None, :] - targets[4][:, None]
    drift_z = src_vel[2][None, :] - targets[5][:, None]
    squared = gap_x * gap_x + gap_y * gap_y + gap_z * gap_z + soft_sq
    inverse = lax.rsqrt(squared)
    weight = mass * inverse * inverse * inverse
    along = 3.0 * (gap_x * drift_x + gap_y * drift_y + gap_z * drift_z) * inverse * inverse
    return jnp.stack(
        [
            jnp.sum(weight * gap_x, axis=1),
            jnp.sum(weight * gap_y, axis=1),
            jnp.sum(weight * gap_z, axis=1),
            jnp.sum(weight * (drift_x - along * gap_x), axis=1),
            jnp.sum(weight * (drift_y - along * gap_y), axis=1),
            jnp.sum(weight * (drift_z - along * gap_z), axis=1),
        ]
    )


def block_terms(packed, src_pos, src_vel, mass, soft_sq):
    width, total = packed.shape
    block = math.gcd(total, 2048)
    grouped = packed.reshape(width, total // block, block).transpose(1, 0, 2)
    result = lax.map(lambda targets: pair_block(targets, src_pos, src_vel, mass, soft_sq), grouped)
    return result.transpose(1, 0, 2).reshape(width, total)


def predict(positions, velocities, accelerations, jerks, elapsed):
    span = elapsed[None, :]
    pred_pos = (
        positions
        + span * velocities
        + 0.5 * span * span * accelerations
        + span * span * span / 6.0 * jerks
    )
    pred_vel = velocities + span * accelerations + 0.5 * span * span * jerks
    return (pred_pos, pred_vel)


def correct(old_pos, old_vel, old_acc, old_jerk, force, jerk_new, span):
    span = span[None, :]
    new_vel = old_vel + 0.5 * span * (old_acc + force) + span * span / 12.0 * (old_jerk - jerk_new)
    new_pos = old_pos + 0.5 * span * (old_vel + new_vel) + span * span / 12.0 * (old_acc - force)
    return (new_pos, new_vel)


def shards(positions, velocities, accelerations, jerks, levels, counts, active_rows):
    n_grp = lax.axis_size("grp")
    n_dev = lax.axis_size("dev")
    g_idx = lax.axis_index("grp")
    d_idx = lax.axis_index("dev")
    devices_all = n_grp * n_dev
    star_dev = positions.shape[1]
    slot_cap = active_rows.shape[1]
    stars_all = star_dev * devices_all
    mass = 1.0 / stars_all
    soft_sq = 0.0004 * (131072.0 / stars_all) ** (2.0 / 3.0)
    row_cap = n_dev * slot_cap
    last_time = -(jnp.left_shift(jnp.int32(1), levels) - 1).astype(jnp.float32) * tick_length
    state = jnp.concatenate([positions, velocities, accelerations, jerks], axis=0)
    for step in range(active_rows.shape[0]):
        now = (step + 1) * tick_length
        pred_pos, pred_vel = predict(state[0:3], state[3:6], state[6:9], state[9:12], now - last_time)
        rows = active_rows[step]
        targets = jnp.concatenate(
            [pred_pos[:, rows], pred_vel[:, rows], jnp.zeros((2, slot_cap), jnp.float32)], axis=0
        ).T
        row_counts = counts[step].reshape(n_grp, n_dev)[g_idx, :]
        packed = targets.reshape(slot_cap * 8 // LANES, LANES)
        copies = lax.optimization_barrier(jnp.broadcast_to(packed[None], (n_dev,) + packed.shape))
        row_targets = lax.all_to_all(copies, "dev", 0, 0, tiled=True).reshape(row_cap, 8)
        mine = jnp.concatenate([pred_pos, pred_vel], axis=0)
        spread = lax.optimization_barrier(jnp.broadcast_to(mine[None], (n_grp,) + mine.shape))
        src = lax.all_to_all(spread, "grp", 0, 0, tiled=True)
        src = src.transpose(1, 0, 2).reshape(6, n_grp * star_dev)
        partial = pair_terms(row_counts, row_targets, src, mass, soft_sq)
        received = lax.all_to_all(partial, "dev", 0, 0, tiled=True)
        own = jnp.sum(received, axis=0)[:6]
        own_count = row_counts[d_idx]
        span = now - last_time[rows]
        old = state[:, rows]
        new_pos, new_vel = correct(old[0:3], old[3:6], old[6:9], old[9:12], own[:3], own[3:], span)
        live = jnp.arange(slot_cap, dtype=jnp.int32) < own_count
        target = jnp.where(live, rows, star_dev)
        state = state.at[:, target].set(jnp.concatenate([new_pos, new_vel, own], axis=0), mode="drop")
        last_time = last_time.at[target].set(now, mode="drop")
    return (state[0:3], state[3:6], state[6:9], state[9:12])


def solution(mesh):
    placed = (
        P(None, ("grp", "dev")),
        P(None, ("grp", "dev")),
        P(None, ("grp", "dev")),
        P(None, ("grp", "dev")),
        P(("grp", "dev")),
        P(),
        P(None, ("grp", "dev")),
    )
    return jax.shard_map(
        shards,
        mesh=mesh,
        in_specs=placed,
        out_specs=(
            P(None, ("grp", "dev")),
            P(None, ("grp", "dev")),
            P(None, ("grp", "dev")),
            P(None, ("grp", "dev")),
        ),
        check_vma=False,
    )
```

profile of v0, /device:TPU:1, one launch (start us, length us, event | category | flops | bytes accessed | tf_op | source)
XLA Modules:
  0.0 376.2 jit_solution(8582961750316073871)
XLA Ops:
  0.6 0.8 slice_reduce_fusion
  1.6 0.6 dynamic_slice.12
  2.2 0.6 dynamic_slice.14
  2.7 2.1 compare_select_fusion
  4.8 0.7 negate_multiply_fusion
  5.5 0.8 multiply_add_fusion.3
  6.5 0.7 gather_fusion.2
  7.6 0.7 gather_fusion.3
  8.8 0.7 broadcast_in_dim.27
  9.5 7.6 %all-to-all-start = ((f32[16,16,128]{2,1,0:T(8,128)}), f32[16,16,128]{2,1,0:T(8,128)S(1)}, u32[]{:S(2)}, u32[]{:S(2)}) async-start(f32[16,16,128]{2,1,0:T(8,128)} %broadcast_in_dim.27), calls=%async_computation | async-start | bytes 262144 | tf_op jit(solution)/shard_map/all_to_all | solution.py:190
  17.0 1.4 gather_fusion.1
  18.4 1.4 scatter_fusion.1
  19.9 0.7 broadcast_in_dim.28
  20.6 0.5 dynamic-slice_bitcast_fusion.1.refs_0_
  21.1 2.8 all-to-all-done
  23.9 7.4 %all-to-all-start.1 = ((f32[8,6,1024]{2,1,0:T(8,128)}), f32[8,6,1024]{2,1,0:T(8,128)S(1)}, u32[]{:S(2)}, u32[]{:S(2)}) async-start(f32[8,6,1024]{2,1,0:T(8,128)} %broadcast_in_dim.28), calls=%async_computation.1 | async-start | bytes 524288 | tf_op jit(solution)/shard_map/all_to_all | solution.py:193
  31.3 2.5 reshape.170.refs_1_
  33.8 4.0 %all-to-all-done.1 = f32[8,6,1024]{2,1,0:T(8,128)S(1)} async-done(((f32[8,6,1024]{2,1,0:T(8,128)}), f32[8,6,1024]{2,1,0:T(8,128)S(1)}, u32[]{:S(2)}, u32[]{:S(2)}) %all-to-all-start.1) | async-done | bytes 196640 | tf_op jit(solution)/shard_map/all_to_all | solution.py:193
  37.8 1.3 broadcast_in_dim.30.refs_2_
  39.1 148.0 %shard_map.102 = f32[16,8,256]{2,1,0:T(8,128)} custom-call(s32[16]{0:T(128)} %dynamic-slice_bitcast_fusion.1.refs_0_, f32[4096,8]{1,0:T(8,128)} %reshape.170.refs_1_, f32[6,8,8192]{2,1,0:T(8,128)} %broadcast_in_dim.30.refs_2_), custom_call_target="tpu_custom_call" | custom-call | tf_op jit(solution)/shard_map/pallas_call | solution.py:102
  187.1 3.5 all-to-all-start.2
  190.9 0.7 gather_fusion
  191.7 5.7 %all-to-all-done.2 = f32[16,8,256]{2,1,0:T(8,128)S(1)} async-done(((f32[16,8,256]{2,1,0:T(8,128)}), f32[16,8,256]{2,1,0:T(8,128)S(1)}, u32[]{:S(2)}, u32[]{:S(2)}) %all-to-all-start.2) | async-done | bytes 131104 | tf_op jit(solution)/shard_map/all_to_all | solution.py:196
  197.6 1.4 scatter_fusion
  198.9 0.5 fusion.11
  200.5 0.7 gather_fusion.6
  201.3 0.2 copy.118
  201.5 0.7 gather_fusion.7
  202.6 0.7 broadcast_in_dim.32
  203.3 3.5 all-to-all-start.3
  206.8 0.7 broadcast_in_dim.33
  207.6 6.1 %all-to-all-done.3 = f32[16,16,128]{2,1,0:T(8,128)S(1)} async-done(((f32[16,16,128]{2,1,0:T(8,128)}), f32[16,16,128]{2,1,0:T(8,128)S(1)}, u32[]{:S(2)}, u32[]{:S(2)}) %all-to-all-start.3) | async-done | bytes 131104 | tf_op jit(solution)/shard_map/all_to_all | solution.py:190
  213.6 3.4 all-to-all-start.4
  217.0 1.4 gather_fusion.5
  218.4 0.5 dynamic-slice_bitcast_fusion.refs_0_
  218.9 2.5 reshape.171.refs_1_
  221.4 0.6 all-to-all-done.4
  221.9 1.3 broadcast_in_dim.35.refs_2_
  223.2 137.4 %shard_map.103 = f32[16,8,256]{2,1,0:T(8,128)} custom-call(s32[16]{0:T(128)} %dynamic-slice_bitcast_fusion.refs_0_, f32[4096,8]{1,0:T(8,128)} %reshape.171.refs_1_, f32[6,8,8192]{2,1,0:T(8,128)} %broadcast_in_dim.35.refs_2_), custom_call_target="tpu_custom_call" | custom-call | tf_op jit(solution)/shard_map/pallas_call | solution.py:102
  360.6 3.5 all-to-all-start.5
  364.2 0.7 gather_fusion.4
  365.0 6.0 %all-to-all-done.5 = f32[16,8,256]{2,1,0:T(8,128)S(1)} async-done(((f32[16,8,256]{2,1,0:T(8,128)}), f32[16,8,256]{2,1,0:T(8,128)S(1)}, u32[]{:S(2)}, u32[]{:S(2)}) %all-to-all-start.5) | async-done | bytes 131104 | tf_op jit(solution)/shard_map/all_to_all | solution.py:196
  371.1 1.4 scatter_fusion.2
  372.5 0.5 fusion.10
  373.0 0.8 copy.123
  373.8 0.8 copy.124
  374.6 0.8 copy.125
  375.4 0.8 copy.126
  (50 shorter events, 3.4 us)
Async XLA Ops:
  9.5 14.5 %all-to-all-start = ((f32[16,16,128]{2,1,0:T(8,128)}), f32[16,16,128]{2,1,0:T(8,128)S(1)}, u32[]{:S(2)}, u32[]{:S(2)}) async-start(f32[16,16,128]{2,1,0:T(8,128)} %broadcast_in_dim.27), calls=%async_computation | async-start | bytes 262144 | tf_op jit(solution)/shard_map/all_to_all | solution.py:190
  23.9 13.9 %all-to-all-start.1 = ((f32[8,6,1024]{2,1,0:T(8,128)}), f32[8,6,1024]{2,1,0:T(8,128)S(1)}, u32[]{:S(2)}, u32[]{:S(2)}) async-start(f32[8,6,1024]{2,1,0:T(8,128)} %broadcast_in_dim.28), calls=%async_computation.1 | async-start | bytes 524288 | tf_op jit(solution)/shard_map/all_to_all | solution.py:193
  39.1 151.5 %copy-start = (f32[3,1024]{1,0:T(4,128)S(1)}, f32[3,1024]{1,0:T(4,128)}, u32[]{:S(2)}) copy-start(f32[3,1024]{1,0:T(4,128)} %param.10) | copy-start | bytes 36868
  39.1 151.5 %copy-start.1 = (f32[3,1024]{1,0:T(4,128)S(1)}, f32[3,1024]{1,0:T(4,128)}, u32[]{:S(2)}) copy-start(f32[3,1024]{1,0:T(4,128)} %param.9) | copy-start | bytes 36868
  39.1 151.5 %copy-start.2 = (f32[3,1024]{1,0:T(4,128)S(1)}, f32[3,1024]{1,0:T(4,128)}, u32[]{:S(2)}) copy-start(f32[3,1024]{1,0:T(4,128)} %param.8) | copy-start | bytes 36868
  39.1 151.5 %copy-start.3 = (f32[3,1024]{1,0:T(4,128)S(1)}, f32[3,1024]{1,0:T(4,128)}, u32[]{:S(2)}) copy-start(f32[3,1024]{1,0:T(4,128)} %param.7) | copy-start | bytes 36868
  187.1 10.3 %all-to-all-start.2 = ((f32[16,8,256]{2,1,0:T(8,128)}), f32[16,8,256]{2,1,0:T(8,128)S(1)}, u32[]{:S(2)}, u32[]{:S(2)}) async-start(f32[16,8,256]{2,1,0:T(8,128)} %shard_map.102), calls=%async_computation.2 | async-start | bytes 262144 | tf_op jit(solution)/shard_map/all_to_all | solution.py:196
  203.3 10.3 %all-to-all-start.3 = ((f32[16,16,128]{2,1,0:T(8,128)}), f32[16,16,128]{2,1,0:T(8,128)S(1)}, u32[]{:S(2)}, u32[]{:S(2)}) async-start(f32[16,16,128]{2,1,0:T(8,128)} %broadcast_in_dim.32), calls=%async_computation.3 | async-start | bytes 262144 | tf_op jit(solution)/shard_map/all_to_all | solution.py:190
  213.6 8.3 %all-to-all-start.4 = ((f32[8,6,1024]{2,1,0:T(8,128)}), f32[8,6,1024]{2,1,0:T(8,128)S(1)}, u32[]{:S(2)}, u32[]{:S(2)}) async-start(f32[8,6,1024]{2,1,0:T(8,128)} %broadcast_in_dim.33), calls=%async_computation.4 | async-start | bytes 524288 | tf_op jit(solution)/shard_map/all_to_all | solution.py:193
  360.6 10.3 %all-to-all-start.5 = ((f32[16,8,256]{2,1,0:T(8,128)}), f32[16,8,256]{2,1,0:T(8,128)S(1)}, u32[]{:S(2)}, u32[]{:S(2)}) async-start(f32[16,8,256]{2,1,0:T(8,128)} %shard_map.103), calls=%async_computation.5 | async-start | bytes 262144 | tf_op jit(solution)/shard_map/all_to_all | solution.py:196
where the time goes:
time: 379 us; the launch traced here: 376 us
  Pallas kernels  285 us (75%)
  local copies, waits for them, and re-layouts  31.9 us (8%)
  starting transfers between devices  28.9 us (8%)
  waiting for transfers between devices  25.1 us (7%)
  other arithmetic  3.88 us (1%)
    pallas_call x2, Pallas kernels, pair_terms(): pl.pallas_call(kernel, out_shape=jax.ShapeDtypeStruct((n_owner, 8, cap //...  285 us
    all_to_all x2, waiting for transfers between devices, shards(): received = lax.all_to_all(partial, 'dev', 0, 0, tiled=True)  11.7 us
    all_to_all x2, starting transfers between devices, shards(): lax.all_to_all(copies, 'dev', 0, 0, tiled=True).reshape(row_cap, 8)  11.1 us
    all_to_all x2, starting transfers between devices, shards(): src = lax.all_to_all(spread, 'grp', 0, 0, tiled=True)  10.7 us
    all_to_all x2, waiting for transfers between devices, shards(): lax.all_to_all(copies, 'dev', 0, 0, tiled=True).reshape(row_cap, 8)  8.87 us
  transfers between devices with their start and end apart: 6, of which 6 were waited for; matrix products, arithmetic and copies ran while one was open for 4% of the time, Pallas kernels for 0%

commit v1 on v0

--- a/solution.py
+++ b/solution.py
@@ -186,10 +186,10 @@
         ).T
         row_counts = counts[step].reshape(n_grp, n_dev)[g_idx, :]
         packed = targets.reshape(slot_cap * 8 // LANES, LANES)
-        copies = lax.optimization_barrier(jnp.broadcast_to(packed[None], (n_dev,) + packed.shape))
+        copies = jnp.broadcast_to(packed[None], (n_dev,) + packed.shape)
         row_targets = lax.all_to_all(copies, "dev", 0, 0, tiled=True).reshape(row_cap, 8)
         mine = jnp.concatenate([pred_pos, pred_vel], axis=0)
-        spread = lax.optimization_barrier(jnp.broadcast_to(mine[None], (n_grp,) + mine.shape))
+        spread = jnp.broadcast_to(mine[None], (n_grp,) + mine.shape)
         src = lax.all_to_all(spread, "grp", 0, 0, tiled=True)
         src = src.transpose(1, 0, 2).reshape(6, n_grp * star_dev)
         partial = pair_terms(row_counts, row_targets, src, mass, soft_sq)

time: 379 us -> 406 us (1.071)
  the two profiles are of different devices: /device:TPU:1 before, /device:TPU:64 now
where the time goes in v1:
time: 406 us; the launch traced here: 405 us
  Pallas kernels  312 us (77%)
  local copies, waits for them, and re-layouts  31.9 us (8%)
  waiting for transfers between devices  28.5 us (7%)
  starting transfers between devices  27.3 us (7%)
    pallas_call x2, Pallas kernels, pair_terms(): pl.pallas_call(kernel, out_shape=jax.ShapeDtypeStruct((n_owner, 8, cap //...  312 us
    all_to_all x2, waiting for transfers between devices, shards(): received = lax.all_to_all(partial, 'dev', 0, 0, tiled=True)  14 us
    all_to_all x2, waiting for transfers between devices, shards(): lax.all_to_all(copies, 'dev', 0, 0, tiled=True).reshape(row_cap, 8)  12.6 us
    all_to_all x2, starting transfers between devices, shards(): lax.all_to_all(copies, 'dev', 0, 0, tiled=True).reshape(row_cap, 8)  10.5 us
    all_to_all x2, starting transfers between devices, shards(): src = lax.all_to_all(spread, 'grp', 0, 0, tiled=True)  9.77 us
  transfers between devices with their start and end apart: 6, of which 5 were waited for; matrix products, arithmetic and copies ran while one was open for 3% of the time, Pallas kernels for 0%

profile of v1, /device:TPU:64, one launch (start us, length us, event | category | flops | bytes accessed | tf_op | source)
XLA Modules:
  0.0 404.5 jit_solution(1215570146667717194)
XLA Ops:
  0.6 0.8 slice_reduce_fusion
  1.6 0.6 dynamic_slice.12
  2.2 0.6 dynamic_slice.14
  2.7 2.1 compare_select_fusion
  4.8 0.7 negate_multiply_fusion
  5.5 0.8 multiply_add_fusion.3
  6.5 0.7 gather_fusion.2
  7.3 0.2 copy.106
  7.6 0.7 gather_fusion.3
  8.8 0.7 broadcast_in_dim.27
  9.5 7.0 %all-to-all-start = ((f32[16,16,128]{2,1,0:T(8,128)}), f32[16,16,128]{2,1,0:T(8,128)S(1)}, u32[]{:S(2)}, u32[]{:S(2)}) async-start(f32[16,16,128]{2,1,0:T(8,128)} %broadcast_in_dim.27), calls=%async_computation | async-start | bytes 262144 | tf_op jit(solution)/shard_map/all_to_all | solution.py:190
  16.5 1.4 gather_fusion.1
  17.9 1.4 scatter_fusion.1
  19.3 0.5 dynamic-slice_bitcast_fusion.1.refs_0_
  19.8 4.6 %all-to-all-done = f32[16,16,128]{2,1,0:T(8,128)S(1)} async-done(((f32[16,16,128]{2,1,0:T(8,128)}), f32[16,16,128]{2,1,0:T(8,128)S(1)}, u32[]{:S(2)}, u32[]{:S(2)}) %all-to-all-start) | async-done | bytes 131104 | tf_op jit(solution)/shard_map/all_to_all | solution.py:190
  24.5 0.7 broadcast_in_dim.28
  25.2 5.0 %all-to-all-start.1 = ((f32[8,6,1024]{2,1,0:T(8,128)}), f32[8,6,1024]{2,1,0:T(8,128)S(1)}, u32[]{:S(2)}, u32[]{:S(2)}) async-start(f32[8,6,1024]{2,1,0:T(8,128)} %broadcast_in_dim.28), calls=%async_computation.1 | async-start | bytes 524288 | tf_op jit(solution)/shard_map/all_to_all | solution.py:193
  30.2 2.5 reshape.170.refs_1_
  32.6 1.9 all-to-all-done.1
  34.6 1.3 broadcast_in_dim.30.refs_2_
  35.8 155.3 %shard_map.102 = f32[16,8,256]{2,1,0:T(8,128)} custom-call(s32[16]{0:T(128)} %dynamic-slice_bitcast_fusion.1.refs_0_, f32[4096,8]{1,0:T(8,128)} %reshape.170.refs_1_, f32[6,8,8192]{2,1,0:T(8,128)} %broadcast_in_dim.30.refs_2_), custom_call_target="tpu_custom_call" | custom-call | tf_op jit(solution)/shard_map/pallas_call | solution.py:102
  191.2 3.5 all-to-all-start.2
  195.0 0.7 gather_fusion
  195.8 6.8 %all-to-all-done.2 = f32[16,8,256]{2,1,0:T(8,128)S(1)} async-done(((f32[16,8,256]{2,1,0:T(8,128)}), f32[16,8,256]{2,1,0:T(8,128)S(1)}, u32[]{:S(2)}, u32[]{:S(2)}) %all-to-all-start.2) | async-done | bytes 131104 | tf_op jit(solution)/shard_map/all_to_all | solution.py:196
  202.8 1.4 scatter_fusion
  204.2 0.5 fusion.11
  205.7 0.7 gather_fusion.6
  206.5 0.2 copy.118
  206.7 0.7 gather_fusion.7
  207.9 0.7 broadcast_in_dim.32
  208.5 3.5 all-to-all-start.3
  212.1 7.9 %all-to-all-done.3 = f32[16,16,128]{2,1,0:T(8,128)S(1)} async-done(((f32[16,16,128]{2,1,0:T(8,128)}), f32[16,16,128]{2,1,0:T(8,128)S(1)}, u32[]{:S(2)}, u32[]{:S(2)}) %all-to-all-start.3) | async-done | bytes 131104 | tf_op jit(solution)/shard_map/all_to_all | solution.py:190
  220.0 0.7 broadcast_in_dim.33
  220.7 4.8 %all-to-all-start.4 = ((f32[8,6,1024]{2,1,0:T(8,128)}), f32[8,6,1024]{2,1,0:T(8,128)S(1)}, u32[]{:S(2)}, u32[]{:S(2)}) async-start(f32[8,6,1024]{2,1,0:T(8,128)} %broadcast_in_dim.33), calls=%async_computation.4 | async-start | bytes 524288 | tf_op jit(solution)/shard_map/all_to_all | solution.py:193
  225.5 1.4 gather_fusion.5
  226.9 0.5 dynamic-slice_bitcast_fusion.refs_0_
  227.4 2.5 reshape.171.refs_1_
  229.9 1.3 broadcast_in_dim.35.refs_2_
  231.2 156.7 %shard_map.103 = f32[16,8,256]{2,1,0:T(8,128)} custom-call(s32[16]{0:T(128)} %dynamic-slice_bitcast_fusion.refs_0_, f32[4096,8]{1,0:T(8,128)} %reshape.171.refs_1_, f32[6,8,8192]{2,1,0:T(8,128)} %broadcast_in_dim.35.refs_2_), custom_call_target="tpu_custom_call" | custom-call | tf_op jit(solution)/shard_map/pallas_call | solution.py:102
  387.8 3.5 all-to-all-start.5
  391.4 0.7 gather_fusion.4
  392.2 7.1 %all-to-all-done.5 = f32[16,8,256]{2,1,0:T(8,128)S(1)} async-done(((f32[16,8,256]{2,1,0:T(8,128)}), f32[16,8,256]{2,1,0:T(8,128)S(1)}, u32[]{:S(2)}, u32[]{:S(2)}) %all-to-all-start.5) | async-done | bytes 131104 | tf_op jit(solution)/shard_map/all_to_all | solution.py:196
  399.5 1.4 scatter_fusion.2
  400.9 0.5 fusion.10
  401.3 0.8 copy.123
  402.1 0.8 copy.124
  402.9 0.8 copy.125
  403.7 0.8 copy.126
  (50 shorter events, 3.2 us)
Async XLA Ops:
  9.5 15.0 %all-to-all-start = ((f32[16,16,128]{2,1,0:T(8,128)}), f32[16,16,128]{2,1,0:T(8,128)S(1)}, u32[]{:S(2)}, u32[]{:S(2)}) async-start(f32[16,16,128]{2,1,0:T(8,128)} %broadcast_in_dim.27), calls=%async_computation | async-start | bytes 262144 | tf_op jit(solution)/shard_map/all_to_all | solution.py:190
  25.2 9.4 %all-to-all-start.1 = ((f32[8,6,1024]{2,1,0:T(8,128)}), f32[8,6,1024]{2,1,0:T(8,128)S(1)}, u32[]{:S(2)}, u32[]{:S(2)}) async-start(f32[8,6,1024]{2,1,0:T(8,128)} %broadcast_in_dim.28), calls=%async_computation.1 | async-start | bytes 524288 | tf_op jit(solution)/shard_map/all_to_all | solution.py:193
  35.8 158.8 %copy-start = (f32[3,1024]{1,0:T(4,128)S(1)}, f32[3,1024]{1,0:T(4,128)}, u32[]{:S(2)}) copy-start(f32[3,1024]{1,0:T(4,128)} %param.10) | copy-start | bytes 36868
  35.8 158.9 %copy-start.1 = (f32[3,1024]{1,0:T(4,128)S(1)}, f32[3,1024]{1,0:T(4,128)}, u32[]{:S(2)}) copy-start(f32[3,1024]{1,0:T(4,128)} %param.9) | copy-start | bytes 36868
  35.8 158.9 %copy-start.2 = (f32[3,1024]{1,0:T(4,128)S(1)}, f32[3,1024]{1,0:T(4,128)}, u32[]{:S(2)}) copy-start(f32[3,1024]{1,0:T(4,128)} %param.8) | copy-start | bytes 36868
  35.8 158.9 %copy-start.3 = (f32[3,1024]{1,0:T(4,128)S(1)}, f32[3,1024]{1,0:T(4,128)}, u32[]{:S(2)}) copy-start(f32[3,1024]{1,0:T(4,128)} %param.7) | copy-start | bytes 36868
  191.2 11.5 %all-to-all-start.2 = ((f32[16,8,256]{2,1,0:T(8,128)}), f32[16,8,256]{2,1,0:T(8,128)S(1)}, u32[]{:S(2)}, u32[]{:S(2)}) async-start(f32[16,8,256]{2,1,0:T(8,128)} %shard_map.102), calls=%async_computation.2 | async-start | bytes 262144 | tf_op jit(solution)/shard_map/all_to_all | solution.py:196
  208.5 11.5 %all-to-all-start.3 = ((f32[16,16,128]{2,1,0:T(8,128)}), f32[16,16,128]{2,1,0:T(8,128)S(1)}, u32[]{:S(2)}, u32[]{:S(2)}) async-start(f32[16,16,128]{2,1,0:T(8,128)} %broadcast_in_dim.32), calls=%async_computation.3 | async-start | bytes 262144 | tf_op jit(solution)/shard_map/all_to_all | solution.py:190
  220.7 9.2 %all-to-all-start.4 = ((f32[8,6,1024]{2,1,0:T(8,128)}), f32[8,6,1024]{2,1,0:T(8,128)S(1)}, u32[]{:S(2)}, u32[]{:S(2)}) async-start(f32[8,6,1024]{2,1,0:T(8,128)} %broadcast_in_dim.33), calls=%async_computation.4 | async-start | bytes 524288 | tf_op jit(solution)/shard_map/all_to_all | solution.py:193
  387.8 11.5 %all-to-all-start.5 = ((f32[16,8,256]{2,1,0:T(8,128)}), f32[16,8,256]{2,1,0:T(8,128)S(1)}, u32[]{:S(2)}, u32[]{:S(2)}) async-start(f32[16,8,256]{2,1,0:T(8,128)} %shard_map.103), calls=%async_computation.5 | async-start | bytes 262144 | tf_op jit(solution)/shard_map/all_to_all | solution.py:196
